TPU v7x, 256 devices: a whole 4x4x8 slice. The times are simulated.
256 devices in a mesh: dp: 4 (over z_hi), expert: 16 (over y, z_lo, core), mp: 4 (over x).
Axes of the slice: x: 4, y: 4, z: 8 (z_hi: 4, z_lo: 2; z = z_hi * 2 + z_lo), core: 2. Of those that a mesh axis runs over, the one named last changes fastest.
Arguments:
- hidden: bfloat16 [16384, 2048], P(('dp', 'expert', 'mp')), may hold values from -6 to 6
- norm_gain: float32 [2048], replicated, may hold values from 0.1 to 1.9
- expert_in: float32 [64, 2048, 2816], P('dp', ('expert', 'mp')), may hold values from -0.125 to 0.125
- expert_out: float32 [64, 2048, 1408], P('dp', ('expert', 'mp')), may hold values from -0.15625 to 0.15625
- expert_ids: int32 [16384, 6], P(('dp', 'expert', 'mp')), may hold values from 0 to 63, all different within a row; in each aligned block of 64 rows (0 to 63, 64 to 127, ...) at most 12 rows name the same one
- gate_levels: int32 [16384, 6], P(('dp', 'expert', 'mp')), may hold values from 1 to 255
- shared_gate: bfloat16 [2048, 2816], P(('dp', 'expert'), 'mp'), may hold values from -0.125 to 0.125
- shared_up: bfloat16 [2048, 2816], P(('dp', 'expert'), 'mp'), may hold values from -0.125 to 0.125
- shared_down: bfloat16 [2048, 2816], P(('dp', 'expert'), 'mp'), may hold values from -0.109375 to 0.109375
- next_gain: float32 [2048], replicated, may hold values from 0.1 to 1.9
- kv_weight: bfloat16 [2048, 576], P(None, 'mp'), may hold values from -0.125 to 0.125
Outputs:
- layer_out: bfloat16 [16384, 2048], P(('dp', 'expert', 'mp'))
- kv_latent: bfloat16 [16384, 576], P(('dp', 'expert'), 'mp')
Inputs may be any that keep to these rules, and one draw needn't show every extreme that they name: `expert_ids`: each row names 6 different experts. Among the 64 rows of one device no expert is named by more than 12 rows, and in every draw some expert is named by exactly 12 rows of some device.
All inputs are finite; a program needn't handle non-finite values.
Results may differ from a plain program's by a relative error of at most 0.012.
Values may be sent and summed in bfloat16 or wider, within the bound.
No kernel may reach another device: no remote copies, remote signals or barrier semaphores. Data moves between devices by JAX's collectives and lax.ppermute only.
A program may use at most 128 MiB of HBM per device.

v0:
```python
import jax
import jax.numpy as jnp
from jax import lax
from jax.sharding import PartitionSpec as P


def rms_scale(values, gain):
    wide = values.astype(jnp.float32)
    mean_sq = jnp.mean(wide * wide, axis=-1, keepdims=True)
    return (wide * lax.rsqrt(mean_sq + 1e-06) * gain).astype(jnp.bfloat16)


def expert_part(rows, gate_up_w, down_w):
    quarter = down_w.shape[1]
    gate_up = jnp.dot(rows, gate_up_w, preferred_element_type=jnp.float32)
    act = (jax.nn.silu(gate_up[:, :quarter]) * gate_up[:, quarter:]).astype(jnp.bfloat16)
    return lax.dot_general(
        act, down_w, (((1,), (1,)), ((), ())), preferred_element_type=jnp.float32
    )


def on_device(
    hidden,
    norm_gain,
    expert_in,
    expert_out,
    expert_ids,
    gate_levels,
    shared_gate,
    shared_up,
    shared_down,
    next_gain,
    kv_weight,
):
    tok_rows, width = hidden.shape
    top = expert_ids.shape[1]
    n_mp = lax.axis_size("mp")
    n_groups = lax.axis_size(("dp", "expert"))
    capacity = min(tok_rows, (2 * tok_rows * top + n_groups - 1) // n_groups)
    local_e, local_rows, double = expert_in.shape
    full_ff = double // 2
    quarter = full_ff // n_mp
    in_cast = (
        expert_in.astype(jnp.bfloat16)
        .reshape(local_e, local_rows, 2, n_mp, quarter)
        .transpose(0, 3, 1, 2, 4)
    )
    out_cast = (
        expert_out.astype(jnp.bfloat16)
        .reshape(local_e, local_rows, n_mp, quarter)
        .transpose(0, 2, 1, 3)
    )
    in_send = in_cast.reshape(local_e * n_mp, local_rows, 2, quarter)
    out_send = out_cast.reshape(local_e * n_mp, local_rows, quarter)
    in_recv, out_recv = (
        lax.all_to_all(in_send, ("expert", "mp"), split_axis=0, concat_axis=1, tiled=True),
        lax.all_to_all(out_send, ("expert", "mp"), split_axis=0, concat_axis=1, tiled=True),
    )
    gate_up_w = in_recv.reshape(width, 2 * quarter)
    down_w = out_recv.reshape(width, quarter)
    normed = rms_scale(hidden, norm_gain)
    levels = gate_levels.astype(jnp.float32)
    gate_weights = levels / jnp.sum(levels, axis=1, keepdims=True)
    flat_ids = expert_ids.reshape(-1)
    pairs = flat_ids.shape[0]
    onehot = (flat_ids[:, None] == jnp.arange(n_groups, dtype=jnp.int32)[None, :]).astype(jnp.int32)
    before = jnp.cumsum(onehot, axis=0) - onehot
    slot_of_pair = jnp.sum(before * onehot, axis=1)
    target = flat_ids * capacity + slot_of_pair
    token_of_pair = jnp.arange(pairs, dtype=jnp.int32) // top
    send = (
        jnp.zeros((n_groups * capacity, width), jnp.bfloat16).at[target].set(normed[token_of_pair])
    )
    received = lax.all_to_all(
        send.reshape(n_groups, capacity, width),
        ("dp", "expert"),
        split_axis=0,
        concat_axis=0,
        tiled=True,
    )
    slots_here = received.reshape(n_groups * capacity, width)
    every_slot = lax.all_gather(slots_here, "mp", axis=0, tiled=True)
    rows = every_slot
    summed = lax.psum_scatter(
        expert_part(rows, gate_up_w, down_w).astype(jnp.bfloat16),
        "mp",
        scatter_dimension=0,
        tiled=True,
    )
    result = summed.reshape(n_groups, capacity, width)
    back = lax.all_to_all(
        result, ("dp", "expert"), split_axis=0, concat_axis=0, tiled=True
    ).reshape(n_groups * capacity, width)
    picked = back[target].reshape(tok_rows, top, width)
    routed = jnp.sum(picked.astype(jnp.float32) * gate_weights[:, :, None], axis=1)
    gate_w, up_w, down_s = (
        lax.all_gather(shared_gate, ("dp", "expert"), axis=0, tiled=True),
        lax.all_gather(shared_up, ("dp", "expert"), axis=0, tiled=True),
        lax.all_gather(shared_down, ("dp", "expert"), axis=0, tiled=True),
    )
    group_rows = lax.all_gather(normed, "mp", axis=0, tiled=True)
    rows = group_rows
    gate_part = jnp.dot(rows, gate_w, preferred_element_type=jnp.float32)
    up_part = jnp.dot(rows, up_w, preferred_element_type=jnp.float32)
    act = (jax.nn.silu(gate_part) * up_part).astype(jnp.bfloat16)
    shared_out = lax.psum_scatter(
        lax.dot_general(act, down_s, (((1,), (1,)), ((), ())), preferred_element_type=jnp.float32),
        "mp",
        scatter_dimension=0,
        tiled=True,
    )
    layer_out = (hidden.astype(jnp.float32) + routed + shared_out).astype(jnp.bfloat16)
    next_rows = rms_scale(layer_out, next_gain)
    next_group = lax.all_gather(next_rows, "mp", axis=0, tiled=True)
    kv_latent = jnp.dot(next_group, kv_weight, preferred_element_type=jnp.float32).astype(
        jnp.bfloat16
    )
    return (layer_out, kv_latent)


def solution(mesh):
    in_specs = (
        P(("dp", "expert", "mp"), None),
        P(),
        P("dp", ("expert", "mp"), None),
        P("dp", ("expert", "mp"), None),
        P(("dp", "expert", "mp"), None),
        P(("dp", "expert", "mp"), None),
        P(("dp", "expert"), "mp"),
        P(("dp", "expert"), "mp"),
        P(("dp", "expert"), "mp"),
        P(),
        P(None, "mp"),
    )
    out_specs = (P(("dp", "expert", "mp"), None), P(("dp", "expert"), "mp"))
    return jax.shard_map(
        on_device, mesh=mesh, in_specs=in_specs, out_specs=out_specs, check_vma=False
    )
```

profile of v0, /device:TPU:1, one launch (start us, length us, event | category | flops | bytes accessed | tf_op | source)
XLA Modules:
  0.0 935.2 jit_solution(4523954897152339868)
XLA Ops:
  7.2 0.0 all-gather.7.cloned.1.call-start
  7.2 0.8 copy.21
  8.1 0.1 eq.29
  8.2 0.1 eq.25
  8.3 0.7 broadcast_multiply_fusion
  9.1 0.9 reduce-window.6
  10.0 0.2 slice_reduce_fusion
  10.2 0.1 copy.20
  10.3 0.1 mul.81
  10.5 1.1 fusion.16
  11.6 0.1 fusion.24
  11.8 1.1 fusion.18
  12.9 10.0 %scatter_custom_fusion = bf16[768,2048]{1,0:T(8,128)(2,1)} fusion(s32[384]{0:T(512)S(1)} %fusion.26, bf16[64,2048]{1,0:T(8,128)(2,1)S(1)} %fusion.18, s32[1024]{0:T(1024)S(1)} %pad_clamp_fusion.1, bf16[]{:T(256)} %constant.12.clone.1), kind=kCustom, calls=%fused_computation.9 | custom fusion | bytes 3145730 | tf_op jit(solution)/shard_map/scatter | solution.py:72
  22.8 6.1 reshape.153
  28.9 108.9 %all_to_all.28 = bf16[64,12,2048]{2,1,0:T(8,128)(2,1)} all-to-all(bf16[64,12,2048]{2,1,0:T(8,128)(2,1)} %reshape.153), channel_id=1, replica_groups=mesh['dp'=4,'expert'=16,'mp'=4] {'dp','expert'}, dimensions={0} | all-to-all | bytes 6291456 | tf_op jit(solution)/shard_map/all_to_all | solution.py:74
  137.8 6.2 reshape.154
  144.0 0.0 all-gather.7.cloned.1.call-update
  144.0 3.0 convert_element_type.54
  147.0 5.1 reshape.155
  152.1 4.8 copy.24
  156.9 9.3 all-to-all-start.1
  166.2 0.2 convert_element_type.56
  166.4 0.5 fusion.31
  166.9 1.4 pad_maximum_fusion
  168.2 54.8 %all-to-all-done.1 = bf16[64,32,2,352]{3,1,2,0:T(8,128)(2,1)} async-done(((bf16[64,32,2,352]{3,1,2,0:T(8,128)(2,1)}), bf16[64,32,2,352]{3,1,2,0:T(8,128)(2,1)}, u32[]{:S(2)}, u32[]{:S(2)}) %all-to-all-start.1) | async-done | bytes 2883616 | tf_op jit(solution)/shard_map/all_to_all | solution.py:56
  223.1 4.4 all-to-all-start.2
  227.4 0.0 reduce-scatter.3.cloned.1.call-start
  227.5 6.9 copy.25
  234.4 7.8 reshape.157
  242.2 70.8 %all-gather.7.cloned.1.call-done = bf16[3072,2048]{1,0:T(8,128)(2,1)} async-done(((bf16[768,2048]{1,0:T(8,128)(2,1)}), bf16[3072,2048]{1,0:T(8,128)(2,1)}) %all-gather.7.cloned.1.call-update) | async-done | bytes 12582928 | tf_op jit(solution)/shard_map/all_gather | solution.py:82
  313.0 15.2 %fusion.32 = f32[3072,704]{0,1:T(8,128)} fusion(bf16[3072,2048]{1,0:T(8,128)(2,1)} %all-gather.7.cloned.1.call-done, bf16[2048,704]{1,0:T(8,128)(2,1)} %reshape.157), kind=kOutput, calls=%fused_computation.62 | convolution fusion | flops 8858370048 | bytes 24117248 | tf_op jit(solution)/shard_map/dot_general | solution.py:15
  328.1 13.5 %convolution_convert_fusion = bf16[3072,2048]{1,0:T(8,128)(2,1)} fusion(bf16[2048,352]{1,0:T(8,128)(2,1)S(1)} %bitcast.36, f32[3072,704]{0,1:T(8,128)} %fusion.32), kind=kOutput, calls=%fused_computation.3 | convolution fusion | flops 4441964544 | bytes 22675456 | tf_op jit(solution)/shard_map/dot_general | solution.py:17
  341.6 0.0 reduce-scatter.3.cloned.1.call-update
  341.6 0.0 all-gather.9.cloned.1.call-start
  341.7 0.7 all-gather.9.cloned.1.call-update
  342.3 0.0 all-gather.11.cloned.1.call-start
  342.4 0.5 all-gather.11.cloned.1.call-update
  342.9 0.0 all-gather.13.cloned.1.call-start
  343.0 0.5 all-gather.13.cloned.1.call-update
  343.5 0.0 all-gather.15.cloned.1.call-start
  343.6 0.5 all-gather.15.cloned.1.call-update
  344.1 115.7 %reduce-scatter.3.cloned.1.call-done = bf16[768,2048]{1,0:T(8,128)(2,1)} async-done(((bf16[3072,2048]{1,0:T(8,128)(2,1)}), bf16[768,2048]{1,0:T(8,128)(2,1)}) %reduce-scatter.3.cloned.1.call-update) | async-done | bytes 3145744 | tf_op jit(solution)/shard_map/reduce_scatter | solution.py:84
  459.8 6.1 reshape.160
  465.9 10.8 %all-to-all-start.3 = ((bf16[64,12,2048]{2,1,0:T(8,128)(2,1)}), bf16[64,12,2048]{2,1,0:T(8,128)(2,1)}, u32[]{:S(2)}, u32[]{:S(2)}) async-start(bf16[64,12,2048]{2,1,0:T(8,128)(2,1)} %reshape.160), calls=%async_computation.4 | async-start | bytes 8388608 | tf_op jit(solution)/shard_map/all_to_all | solution.py:91
  476.8 0.3 reduce-scatter.5.cloned.1.call-start
  477.0 10.5 %all-gather.9.cloned.1.call-done = bf16[256,2048]{1,0:T(8,128)(2,1)} async-done(((bf16[64,2048]{1,0:T(8,128)(2,1)}), bf16[256,2048]{1,0:T(8,128)(2,1)}) %all-gather.9.cloned.1.call-update) | async-done | bytes 1048592 | tf_op jit(solution)/shard_map/all_gather | solution.py:101
  487.6 139.0 %all-gather.11.cloned.1.call-done = bf16[2048,704]{1,0:T(8,128)(2,1)} async-done(((bf16[32,704]{1,0:T(8,128)(2,1)}), bf16[2048,704]{1,0:T(8,128)(2,1)}) %all-gather.11.cloned.1.call-update) | async-done | bytes 2883600 | tf_op jit(solution)/shard_map/all_gather | solution.py:97
  626.6 3.5 fusion.33
  630.1 114.3 %all-gather.13.cloned.1.call-done = bf16[2048,704]{1,0:T(8,128)(2,1)} async-done(((bf16[32,704]{1,0:T(8,128)(2,1)}), bf16[2048,704]{1,0:T(8,128)(2,1)}) %all-gather.13.cloned.1.call-update) | async-done | bytes 2883600 | tf_op jit(solution)/shard_map/all_gather | solution.py:98
  744.4 115.5 %all-gather.15.cloned.1.call-done = bf16[2048,704]{1,0:T(8,128)(2,1)} async-done(((bf16[32,704]{1,0:T(8,128)(2,1)}), bf16[2048,704]{1,0:T(8,128)(2,1)}) %all-gather.15.cloned.1.call-update) | async-done | bytes 2883600 | tf_op jit(solution)/shard_map/all_gather | solution.py:99
  860.0 7.6 fusion.7
  867.6 0.0 reduce-scatter.5.cloned.1.call-update
  867.6 0.0 all-gather.17.cloned.1.call-start
  867.7 0.1 copy.26
  867.8 6.2 reshape.161
  874.0 6.7 gather_fusion
  880.7 2.2 reshape.162
  882.8 3.8 multiply_reduce_fusion
  886.7 11.5 %reduce-scatter.5.cloned.1.call-done = f32[64,2048]{1,0:T(8,128)} async-done(((f32[256,2048]{1,0:T(8,128)}), f32[64,2048]{1,0:T(8,128)}) %reduce-scatter.5.cloned.1.call-update) | async-done | bytes 524304 | tf_op jit(solution)/shard_map/reduce_scatter | solution.py:106
  898.2 1.2 fusion.13
  899.4 0.8 fusion.15
  900.3 0.0 all-gather.17.cloned.1.call-update
  900.3 25.5 %all-gather.17.cloned.1.call-done = bf16[256,2048]{1,0:T(8,128)(2,1)} async-done(((bf16[64,2048]{1,0:T(8,128)(2,1)}), bf16[256,2048]{1,0:T(8,128)(2,1)}) %all-gather.17.cloned.1.call-update) | async-done | bytes 1048592 | tf_op jit(solution)/shard_map/all_gather | solution.py:114
  925.8 2.4 convolution_convert_fusion.1
  (28 shorter events, 0.2 us)
Async XLA Ops:
  7.2 918.6 %copy-start = (bf16[2048,144]{0,1:T(8,128)(2,1)S(1)}, bf16[2048,144]{0,1:T(8,128)(2,1)}, u32[]{:S(2)}) copy-start(bf16[2048,144]{0,1:T(8,128)(2,1)} %param.21) | copy-start | bytes 1769476
  7.2 305.8 %all-gather.7.cloned.1.call-start = ((), (), s32[]{:S(2)}) async-start(), calls=%async_computation.6 | async-start | bytes 15728640 | tf_op jit(solution)/shard_map/all_gather | solution.py:82
  12.9 16.1 %copy-start.3 = (bf16[64,2048]{1,0:T(8,128)(2,1)}, bf16[64,2048]{1,0:T(8,128)(2,1)S(1)}, u32[]{:S(2)}) copy-start(bf16[64,2048]{1,0:T(8,128)(2,1)S(1)} %fusion.18) | copy-start | bytes 786436
  156.9 9.3 copy-start.1
  156.9 66.2 %all-to-all-start.1 = ((bf16[64,32,2,352]{3,1,2,0:T(8,128)(2,1)}), bf16[64,32,2,352]{3,1,2,0:T(8,128)(2,1)}, u32[]{:S(2)}, u32[]{:S(2)}) async-start(bf16[64,32,2,352]{3,1,2,0:T(8,128)(2,1)} %bitcast.34), calls=%async_computation.1 | async-start | bytes 6291456 | tf_op jit(solution)/shard_map/all_to_all | solution.py:56
  223.1 105.1 %all-to-all-start.2 = ((bf16[64,32,352]{2,1,0:T(8,128)(2,1)}), bf16[64,32,352]{2,1,0:T(8,128)(2,1)S(1)}, u32[]{:S(2)}, u32[]{:S(2)}) async-start(bf16[64,32,352]{2,1,0:T(8,128)(2,1)} %bitcast.3), calls=%async_computation.2 | async-start | bytes 3145728 | tf_op jit(solution)/shard_map/all_to_all | solution.py:57
  227.4 232.4 %reduce-scatter.3.cloned.1.call-start = ((), (), s32[]{:S(2)}) async-start(), calls=%async_computation.7 | async-start | bytes 15728640 | tf_op jit(solution)/shard_map/reduce_scatter | solution.py:84
  341.6 146.0 %all-gather.9.cloned.1.call-start = ((), (), s32[]{:S(2)}) async-start(), calls=%async_computation.8 | async-start | bytes 1310720 | tf_op jit(solution)/shard_map/all_gather | solution.py:101
  342.3 284.3 %all-gather.11.cloned.1.call-start = ((), (), s32[]{:S(2)}) async-start(), calls=%async_computation.9 | async-start | bytes 3194880 | tf_op jit(solution)/shard_map/all_gather | solution.py:97
  342.9 401.5 %all-gather.13.cloned.1.call-start = ((), (), s32[]{:S(2)}) async-start(), calls=%async_computation.10 | async-start | bytes 3194880 | tf_op jit(solution)/shard_map/all_gather | solution.py:98
  343.5 516.4 %all-gather.15.cloned.1.call-start = ((), (), s32[]{:S(2)}) async-start(), calls=%async_computation.11 | async-start | bytes 3194880 | tf_op jit(solution)/shard_map/all_gather | solution.py:99
  465.9 401.9 %all-to-all-start.3 = ((bf16[64,12,2048]{2,1,0:T(8,128)(2,1)}), bf16[64,12,2048]{2,1,0:T(8,128)(2,1)}, u32[]{:S(2)}, u32[]{:S(2)}) async-start(bf16[64,12,2048]{2,1,0:T(8,128)(2,1)} %reshape.160), calls=%async_computation.4 | async-start | bytes 8388608 | tf_op jit(solution)/shard_map/all_to_all | solution.py:91
  476.8 421.4 %reduce-scatter.5.cloned.1.call-start = ((), (), s32[]{:S(2)}) async-start(), calls=%async_computation.12 | async-start | bytes 2621440 | tf_op jit(solution)/shard_map/reduce_scatter | solution.py:106
  487.6 372.4 %copy-start.7 = (bf16[256,2048]{1,0:T(8,128)(2,1)S(1)}, bf16[256,2048]{1,0:T(8,128)(2,1)}, u32[]{:S(2)}) copy-start(bf16[256,2048]{1,0:T(8,128)(2,1)} %all-gather.9.cloned.1.call-done) | copy-start | bytes 3145732
  630.1 237.5 %copy-start.5 = (s32[64,6]{0,1:T(8,128)S(1)}, s32[64,6]{0,1:T(8,128)}, u32[]{:S(2)}) copy-start(s32[64,6]{0,1:T(8,128)} %param.16) | copy-start | bytes 4612
  867.6 58.2 %all-gather.17.cloned.1.call-start = ((), (), s32[]{:S(2)}) async-start(), calls=%async_computation.13 | async-start | bytes 1310720 | tf_op jit(solution)/shard_map/all_gather | solution.py:114
  882.8 15.3 %copy-start.2 = (bf16[64,2048]{1,0:T(8,128)(2,1)S(1)}, bf16[64,2048]{1,0:T(8,128)(2,1)}, u32[]{:S(2)}) copy-start(bf16[64,2048]{1,0:T(8,128)(2,1)} %param.11) | copy-start | bytes 786436
  882.8 16.6 %copy-start.6 = (f32[2048]{0:T(1024)S(1)}, f32[2048]{0:T(1024)}, u32[]{:S(2)}) copy-start(f32[2048]{0:T(1024)} %param.20) | copy-start | bytes 24580
  899.4 28.7 %copy-start.4 = (bf16[64,2048]{1,0:T(8,128)(2,1)}, bf16[64,2048]{1,0:T(8,128)(2,1)S(1)}, u32[]{:S(2)}) copy-start(bf16[64,2048]{1,0:T(8,128)(2,1)S(1)} %get-tuple-element.3) | copy-start | bytes 786436
Sparse Core Ops, SparseCore 0:
  144.1 168.7 all-gather.6
  341.7 118.0 reduce-scatter.2
  462.2 25.2 all-gather.8
  489.3 137.2 all-gather.10
  628.3 116.0 all-gather.12
  746.1 113.7 all-gather.14
  867.7 30.4 reduce-scatter.4
  900.4 25.2 all-gather.16
where the time goes:
time: 945 us; the launch traced here: 935 us
  waiting for transfers between devices  660 us (70%)
  blocking collectives  109 us (12%)
  local copies, waits for them, and re-layouts  70.1 us (7%)
  matrix products  42.1 us (4%)
  starting transfers between devices  25.1 us (3%)
  between operations  14.6 us (2%)
  other arithmetic  14.5 us (2%)
    all_gather x1, waiting for transfers between devices, on_device(): lax.all_gather(shared_gate, ('dp', 'expert'), axis=0, tiled=True)  139 us
    reduce_scatter x1, waiting for transfers between devices, on_device(): lax.psum_scatter(expert_part(rows, gate_up_w, down_w).astype(jnp.bfloat16...  116 us
    all_gather x1, waiting for transfers between devices, on_device(): lax.all_gather(shared_down, ('dp', 'expert'), axis=0, tiled=True)  116 us
    all_gather x1, waiting for transfers between devices, on_device(): lax.all_gather(shared_up, ('dp', 'expert'), axis=0, tiled=True)  114 us
    all_to_all x1, blocking collectives, on_device(): lax.all_to_all(send.reshape(n_groups, capacity, width), ('dp', 'expert'),...  109 us
    all_gather x1, waiting for transfers between devices, on_device(): every_slot = lax.all_gather(slots_here, 'mp', axis=0, tiled=True)  70.8 us
    all_to_all x1, waiting for transfers between devices, on_device(): lax.all_to_all(in_send, ('expert', 'mp'), split_axis=0, concat_axis=1, ti...  54.8 us
    all_gather x1, waiting for transfers between devices, on_device(): next_group = lax.all_gather(next_rows, 'mp', axis=0, tiled=True)  25.5 us
  transfers between devices with their start and end apart: 11, of which 9 were waited for; matrix products, arithmetic and copies ran while one was open for 9% of the time, Pallas kernels for 0%

commit v1 on v0

--- a/solution.py
+++ b/solution.py
@@ -53,7 +53,15 @@
     in_send = in_cast.reshape(local_e * n_mp, local_rows, 2, quarter)
     out_send = out_cast.reshape(local_e * n_mp, local_rows, quarter)
     in_recv, out_recv = (
-        lax.all_to_all(in_send, ("expert", "mp"), split_axis=0, concat_axis=1, tiled=True),
+        jnp.concatenate(
+            lax.all_to_all(
+                jnp.stack(jnp.split(in_send, lax.axis_size(("expert", "mp")), axis=0)),
+                ("expert", "mp"),
+                0,
+                0,
+            ),
+            axis=1,
+        ),
         lax.all_to_all(out_send, ("expert", "mp"), split_axis=0, concat_axis=1, tiled=True),
     )
     gate_up_w = in_recv.reshape(width, 2 * quarter)

time: 945 us -> 946 us (level)
  blocking collectives: 109 us -> 0 us
  local copies, waits for them, and re-layouts: 70.1 us -> 152 us
  starting transfers between devices: 25.1 us -> 40 us
  waiting for transfers between devices: 660 us -> 670 us
    all_to_all x1 -> x0, blocking collectives: 109 us -> none  [on_device(): lax.all_to_all(send.reshape(n_groups, capacity, width), ('dp', 'expert'),...]
    unnamed x17 -> x82, local copies, waits for them, and re-layouts: 0.87 us -> 83.5 us
    all_to_all x1 -> x2, waiting for transfers between devices: 54.8 us -> 132 us  [the longest x1 76.8 us: on_device(): lax.all_to_all(send.reshape(n_groups, capacity, width), ('dp', 'expert'),...]
    all_gather x1, waiting for transfers between devices: 70.8 us -> 0.01 us  [on_device(): every_slot = lax.all_gather(slots_here, 'mp', axis=0, tiled=True)]
    all_to_all x1 -> x2, starting transfers between devices: 9.32 us -> 23.8 us  [the longest x1 13.3 us: on_device(): lax.all_to_all(send.reshape(n_groups, capacity, width), ('dp', 'expert'),...]
  transfers between devices with their start and end apart: 11 -> 12, of which waited for: 9 -> 9; matrix products, arithmetic and copies ran while one was open for 9% -> 17% of each run, Pallas kernels for 0% -> 0%
where the time goes in v1:
time: 946 us; the launch traced here: 933 us
  waiting for transfers between devices  670 us (71%)
  local copies, waits for them, and re-layouts  152 us (16%)
  matrix products  42.1 us (4%)
  starting transfers between devices  40 us (4%)
  between operations  14.6 us (2%)
  other arithmetic  14.5 us (2%)
    all_gather x1, waiting for transfers between devices, on_device(): lax.all_gather(shared_gate, ('dp', 'expert'), axis=0, tiled=True)  139 us
    reduce_scatter x1, waiting for transfers between devices, on_device(): lax.psum_scatter(expert_part(rows, gate_up_w, down_w).astype(jnp.bfloat16...  120 us
    all_gather x1, waiting for transfers between devices, on_device(): lax.all_gather(shared_down, ('dp', 'expert'), axis=0, tiled=True)  116 us
    all_gather x1, waiting for transfers between devices, on_device(): lax.all_gather(shared_up, ('dp', 'expert'), axis=0, tiled=True)  114 us
    unnamed x82, local copies, waits for them, and re-layouts  83.5 us
    all_to_all x1, waiting for transfers between devices, on_device(): lax.all_to_all(send.reshape(n_groups, capacity, width), ('dp', 'expert'),...  76.8 us
    all_to_all x1, waiting for transfers between devices, on_device(): lax.all_to_all(jnp.stack(jnp.split(in_send, lax.axis_size(('expert', 'mp'...  54.8 us
    all_gather x1, waiting for transfers between devices, on_device(): next_group = lax.all_gather(next_rows, 'mp', axis=0, tiled=True)  25.5 us
  transfers between devices with their start and end apart: 12, of which 9 were waited for; matrix products, arithmetic and copies ran while one was open for 17% of the time, Pallas kernels for 0%

profile of v1, /device:TPU:1, one launch (start us, length us, event | category | flops | bytes accessed | tf_op | source)
XLA Modules:
  0.0 933.1 jit_solution(978506361413794132)
XLA Ops:
  12.8 9.9 %scatter_custom_fusion = bf16[768,2048]{1,0:T(8,128)(2,1)} fusion(s32[384]{0:T(512)S(1)} %fusion.26, bf16[64,2048]{1,0:T(8,128)(2,1)S(1)} %fusion.18, s32[1024]{0:T(1024)S(1)} %pad_clamp_fusion.1, bf16[]{:T(256)} %constant.12.clone.1), kind=kCustom, calls=%fused_computation.9 | custom fusion | bytes 3145730 | tf_op jit(solution)/shard_map/scatter | solution.py:80
  22.8 6.1 reshape.146
  28.9 13.3 %all-to-all-start = ((bf16[64,12,2048]{2,1,0:T(8,128)(2,1)}), bf16[64,12,2048]{2,1,0:T(8,128)(2,1)}, u32[]{:S(2)}, u32[]{:S(2)}) async-start(bf16[64,12,2048]{2,1,0:T(8,128)(2,1)} %reshape.146), calls=%async_computation | async-start | bytes 8388608 | tf_op jit(solution)/shard_map/all_to_all | solution.py:82
  42.8 3.0 convert_element_type.54
  45.8 5.0 reshape.148
  50.8 2.6 copy.24
  59.5 76.8 %all-to-all-done = bf16[64,12,2048]{2,1,0:T(8,128)(2,1)} async-done(((bf16[64,12,2048]{2,1,0:T(8,128)(2,1)}), bf16[64,12,2048]{2,1,0:T(8,128)(2,1)}, u32[]{:S(2)}, u32[]{:S(2)}) %all-to-all-start) | async-done | bytes 3145760 | tf_op jit(solution)/shard_map/all_to_all | solution.py:82
  136.3 6.1 reshape.147
  143.8 1.4 constant_dynamic-update-slice_fusion.53
  146.7 1.4 constant_dynamic-update-slice_fusion.51
  148.1 1.4 constant_dynamic-update-slice_fusion.50
  149.5 1.4 constant_dynamic-update-slice_fusion.49
  153.8 1.4 constant_dynamic-update-slice_fusion.46
  155.2 1.4 constant_dynamic-update-slice_fusion.45
  156.6 1.4 constant_dynamic-update-slice_fusion.44
  158.0 1.4 constant_dynamic-update-slice_fusion.43
  159.5 1.4 constant_dynamic-update-slice_fusion.42
  160.9 1.4 constant_dynamic-update-slice_fusion.41
  162.3 1.4 constant_dynamic-update-slice_fusion.40
  166.6 1.4 constant_dynamic-update-slice_fusion.37
  168.0 1.4 constant_dynamic-update-slice_fusion.36
  175.1 1.4 constant_dynamic-update-slice_fusion.31
  182.2 1.4 constant_dynamic-update-slice_fusion.26
  183.6 1.4 constant_dynamic-update-slice_fusion.25
  185.0 1.4 constant_dynamic-update-slice_fusion.24
  187.8 1.4 constant_dynamic-update-slice_fusion.22
  193.5 1.4 constant_dynamic-update-slice_fusion.18
  196.3 1.4 constant_dynamic-update-slice_fusion.16
  197.8 1.4 constant_dynamic-update-slice_fusion.15
  199.2 1.4 constant_dynamic-update-slice_fusion.14
  200.6 1.4 constant_dynamic-update-slice_fusion.13
  203.4 1.4 constant_dynamic-update-slice_fusion.11
  204.9 1.4 constant_dynamic-update-slice_fusion.10
  206.3 1.4 constant_dynamic-update-slice_fusion.9
  209.1 1.4 constant_dynamic-update-slice_fusion.7
  210.5 1.4 constant_dynamic-update-slice_fusion.6
  212.0 1.4 constant_dynamic-update-slice_fusion.5
  213.4 1.4 constant_dynamic-update-slice_fusion.4
  214.8 1.4 constant_dynamic-update-slice_fusion.3
  217.6 1.4 constant_dynamic-update-slice_fusion.1
  219.1 1.4 constant_dynamic-update-slice_fusion
  220.5 10.4 %all-to-all-start.1 = ((bf16[64,1,32,2,352]{4,2,3,1,0:T(8,128)(2,1)}), bf16[64,1,32,2,352]{4,2,3,1,0:T(8,128)(2,1)}, u32[]{:S(2)}, u32[]{:S(2)}) async-start(bf16[64,1,32,2,352]{4,2,3,1,0:T(8,128)(2,1)} %constant_dynamic-update-slice_fusion), calls=%async_computation.1 | async-start | bytes 6291456 | tf_op jit(solution)/shard_map/all_to_all | solution.py:57
  232.9 54.8 %all-to-all-done.1 = bf16[64,1,32,2,352]{4,2,3,1,0:T(8,128)(2,1)} async-done(((bf16[64,1,32,2,352]{4,2,3,1,0:T(8,128)(2,1)}), bf16[64,1,32,2,352]{4,2,3,1,0:T(8,128)(2,1)}, u32[]{:S(2)}, u32[]{:S(2)}) %all-to-all-start.1) | async-done | bytes 2883616 | tf_op jit(solution)/shard_map/all_to_all | solution.py:57
  287.8 4.4 all-to-all-start.2
  292.2 6.9 copy.25
  299.1 7.8 reshape_reshape.3
  306.9 15.2 %fusion.32 = f32[3072,704]{0,1:T(8,128)} fusion(bf16[3072,2048]{1,0:T(8,128)(2,1)} %all-gather.7.cloned.1.call-done, bf16[2048,704]{1,0:T(8,128)(2,1)} %reshape_reshape.3), kind=kOutput, calls=%fused_computation.190 | convolution fusion | flops 8858370048 | bytes 24117248 | tf_op jit(solution)/shard_map/dot_general | solution.py:15
  322.1 13.5 %convolution_convert_fusion = bf16[3072,2048]{1,0:T(8,128)(2,1)} fusion(bf16[2048,352]{1,0:T(8,128)(2,1)S(1)} %bitcast.357, f32[3072,704]{0,1:T(8,128)} %fusion.32), kind=kOutput, calls=%fused_computation.3 | convolution fusion | flops 4441964544 | bytes 22675456 | tf_op jit(solution)/shard_map/dot_general | solution.py:17
  338.0 120.1 %reduce-scatter.3.cloned.1.call-done = bf16[768,2048]{1,0:T(8,128)(2,1)} async-done(((bf16[3072,2048]{1,0:T(8,128)(2,1)}), bf16[768,2048]{1,0:T(8,128)(2,1)}) %reduce-scatter.3.cloned.1.call-update) | async-done | bytes 3145744 | tf_op jit(solution)/shard_map/reduce_scatter | solution.py:92
  458.1 6.1 reshape.152
  464.3 10.8 %all-to-all-start.3 = ((bf16[64,12,2048]{2,1,0:T(8,128)(2,1)}), bf16[64,12,2048]{2,1,0:T(8,128)(2,1)}, u32[]{:S(2)}, u32[]{:S(2)}) async-start(bf16[64,12,2048]{2,1,0:T(8,128)(2,1)} %reshape.152), calls=%async_computation.4 | async-start | bytes 8388608 | tf_op jit(solution)/shard_map/all_to_all | solution.py:99
  475.4 10.5 %all-gather.9.cloned.1.call-done = bf16[256,2048]{1,0:T(8,128)(2,1)} async-done(((bf16[64,2048]{1,0:T(8,128)(2,1)}), bf16[256,2048]{1,0:T(8,128)(2,1)}) %all-gather.9.cloned.1.call-update) | async-done | bytes 1048592 | tf_op jit(solution)/shard_map/all_gather | solution.py:109
  485.9 138.9 %all-gather.11.cloned.1.call-done = bf16[2048,704]{1,0:T(8,128)(2,1)} async-done(((bf16[32,704]{1,0:T(8,128)(2,1)}), bf16[2048,704]{1,0:T(8,128)(2,1)}) %all-gather.11.cloned.1.call-update) | async-done | bytes 2883600 | tf_op jit(solution)/shard_map/all_gather | solution.py:105
  624.8 3.5 fusion.33
  628.4 114.0 %all-gather.13.cloned.1.call-done = bf16[2048,704]{1,0:T(8,128)(2,1)} async-done(((bf16[32,704]{1,0:T(8,128)(2,1)}), bf16[2048,704]{1,0:T(8,128)(2,1)}) %all-gather.13.cloned.1.call-update) | async-done | bytes 2883600 | tf_op jit(solution)/shard_map/all_gather | solution.py:106
  742.3 115.5 %all-gather.15.cloned.1.call-done = bf16[2048,704]{1,0:T(8,128)(2,1)} async-done(((bf16[32,704]{1,0:T(8,128)(2,1)}), bf16[2048,704]{1,0:T(8,128)(2,1)}) %all-gather.15.cloned.1.call-update) | async-done | bytes 2883600 | tf_op jit(solution)/shard_map/all_gather | solution.py:107
  857.9 7.6 fusion.7
  865.7 6.2 reshape.153
  871.9 6.7 gather_fusion
  878.6 2.2 reshape.154
  880.8 3.8 multiply_reduce_fusion
  884.6 11.5 %reduce-scatter.5.cloned.1.call-done = f32[64,2048]{1,0:T(8,128)} async-done(((f32[256,2048]{1,0:T(8,128)}), f32[64,2048]{1,0:T(8,128)}) %reduce-scatter.5.cloned.1.call-update) | async-done | bytes 524304 | tf_op jit(solution)/shard_map/reduce_scatter | solution.py:114
  898.2 25.5 %all-gather.17.cloned.1.call-done = bf16[256,2048]{1,0:T(8,128)(2,1)} async-done(((bf16[64,2048]{1,0:T(8,128)(2,1)}), bf16[256,2048]{1,0:T(8,128)(2,1)}) %all-gather.17.cloned.1.call-update) | async-done | bytes 1048592 | tf_op jit(solution)/shard_map/all_gather | solution.py:122
  923.7 2.4 convolution_convert_fusion.1
  (95 shorter events, 50.3 us)
Async XLA Ops:
  7.2 916.5 %copy-start = (bf16[2048,144]{0,1:T(8,128)(2,1)S(1)}, bf16[2048,144]{0,1:T(8,128)(2,1)}, u32[]{:S(2)}) copy-start(bf16[2048,144]{0,1:T(8,128)(2,1)} %param.21) | copy-start | bytes 1769476
  12.8 16.1 %copy-start.4 = (bf16[64,2048]{1,0:T(8,128)(2,1)}, bf16[64,2048]{1,0:T(8,128)(2,1)S(1)}, u32[]{:S(2)}) copy-start(bf16[64,2048]{1,0:T(8,128)(2,1)S(1)} %fusion.18) | copy-start | bytes 786436
  28.9 107.4 %all-to-all-start = ((bf16[64,12,2048]{2,1,0:T(8,128)(2,1)}), bf16[64,12,2048]{2,1,0:T(8,128)(2,1)}, u32[]{:S(2)}, u32[]{:S(2)}) async-start(bf16[64,12,2048]{2,1,0:T(8,128)(2,1)} %reshape.146), calls=%async_computation | async-start | bytes 8388608 | tf_op jit(solution)/shard_map/all_to_all | solution.py:82
  42.2 264.7 %all-gather.7.cloned.1.call-start = ((), (), s32[]{:S(2)}) async-start(), calls=%async_computation.6 | async-start | bytes 15728640 | tf_op jit(solution)/shard_map/all_gather | solution.py:90
  53.4 5.4 copy-start.1
  220.5 10.5 %copy-start.2 = (f32[16,32,1408]{2,1,0:T(8,128)S(1)}, f32[16,32,1408]{2,1,0:T(8,128)}, u32[]{:S(2)}) copy-start(f32[16,32,1408]{2,1,0:T(8,128)} %param.14) | copy-start | bytes 8650756
  220.5 67.3 %all-to-all-start.1 = ((bf16[64,1,32,2,352]{4,2,3,1,0:T(8,128)(2,1)}), bf16[64,1,32,2,352]{4,2,3,1,0:T(8,128)(2,1)}, u32[]{:S(2)}, u32[]{:S(2)}) async-start(bf16[64,1,32,2,352]{4,2,3,1,0:T(8,128)(2,1)} %constant_dynamic-update-slice_fusion), calls=%async_computation.1 | async-start | bytes 6291456 | tf_op jit(solution)/shard_map/all_to_all | solution.py:57
  287.8 34.3 %all-to-all-start.2 = ((bf16[64,32,352]{2,1,0:T(8,128)(2,1)}), bf16[64,32,352]{2,1,0:T(8,128)(2,1)S(1)}, u32[]{:S(2)}, u32[]{:S(2)}) async-start(bf16[64,32,352]{2,1,0:T(8,128)(2,1)} %bitcast.67), calls=%async_computation.2 | async-start | bytes 3145728 | tf_op jit(solution)/shard_map/all_to_all | solution.py:65
  292.2 166.0 %reduce-scatter.3.cloned.1.call-start = ((), (), s32[]{:S(2)}) async-start(), calls=%async_computation.7 | async-start | bytes 15728640 | tf_op jit(solution)/shard_map/reduce_scatter | solution.py:92
  335.6 150.3 %all-gather.9.cloned.1.call-start = ((), (), s32[]{:S(2)}) async-start(), calls=%async_computation.8 | async-start | bytes 1310720 | tf_op jit(solution)/shard_map/all_gather | solution.py:109
  336.3 288.5 %all-gather.11.cloned.1.call-start = ((), (), s32[]{:S(2)}) async-start(), calls=%async_computation.9 | async-start | bytes 3194880 | tf_op jit(solution)/shard_map/all_gather | solution.py:105
  336.9 405.5 %all-gather.13.cloned.1.call-start = ((), (), s32[]{:S(2)}) async-start(), calls=%async_computation.10 | async-start | bytes 3194880 | tf_op jit(solution)/shard_map/all_gather | solution.py:106
  337.5 520.4 %all-gather.15.cloned.1.call-start = ((), (), s32[]{:S(2)}) async-start(), calls=%async_computation.11 | async-start | bytes 3194880 | tf_op jit(solution)/shard_map/all_gather | solution.py:107
  464.3 401.5 %all-to-all-start.3 = ((bf16[64,12,2048]{2,1,0:T(8,128)(2,1)}), bf16[64,12,2048]{2,1,0:T(8,128)(2,1)}, u32[]{:S(2)}, u32[]{:S(2)}) async-start(bf16[64,12,2048]{2,1,0:T(8,128)(2,1)} %reshape.152), calls=%async_computation.4 | async-start | bytes 8388608 | tf_op jit(solution)/shard_map/all_to_all | solution.py:99
  475.1 421.0 %reduce-scatter.5.cloned.1.call-start = ((), (), s32[]{:S(2)}) async-start(), calls=%async_computation.12 | async-start | bytes 2621440 | tf_op jit(solution)/shard_map/reduce_scatter | solution.py:114
  485.9 372.0 %copy-start.8 = (bf16[256,2048]{1,0:T(8,128)(2,1)S(1)}, bf16[256,2048]{1,0:T(8,128)(2,1)}, u32[]{:S(2)}) copy-start(bf16[256,2048]{1,0:T(8,128)(2,1)} %all-gather.9.cloned.1.call-done) | copy-start | bytes 3145732
  628.4 237.2 %copy-start.6 = (s32[64,6]{0,1:T(8,128)S(1)}, s32[64,6]{0,1:T(8,128)}, u32[]{:S(2)}) copy-start(s32[64,6]{0,1:T(8,128)} %param.16) | copy-start | bytes 4612
  865.5 58.2 %all-gather.17.cloned.1.call-start = ((), (), s32[]{:S(2)}) async-start(), calls=%async_computation.13 | async-start | bytes 1310720 | tf_op jit(solution)/shard_map/all_gather | solution.py:122
  880.8 15.3 %copy-start.3 = (bf16[64,2048]{1,0:T(8,128)(2,1)S(1)}, bf16[64,2048]{1,0:T(8,128)(2,1)}, u32[]{:S(2)}) copy-start(bf16[64,2048]{1,0:T(8,128)(2,1)} %param.11) | copy-start | bytes 786436
  880.8 16.6 %copy-start.7 = (f32[2048]{0:T(1024)S(1)}, f32[2048]{0:T(1024)}, u32[]{:S(2)}) copy-start(f32[2048]{0:T(1024)} %param.20) | copy-start | bytes 24580
  897.3 28.7 %copy-start.5 = (bf16[64,2048]{1,0:T(8,128)(2,1)}, bf16[64,2048]{1,0:T(8,128)(2,1)S(1)}, u32[]{:S(2)}) copy-start(bf16[64,2048]{1,0:T(8,128)(2,1)S(1)} %get-tuple-element.3) | copy-start | bytes 786436
Sparse Core Ops, SparseCore 0:
  142.5 153.7 all-gather.6
  335.7 122.3 reduce-scatter.2
  460.5 25.3 all-gather.8
  487.6 137.1 all-gather.10
  626.5 115.7 all-gather.12
  744.1 113.7 all-gather.14
  865.6 30.4 reduce-scatter.4
  898.3 25.2 all-gather.16
